TPU v7x, 256 devices: a whole 4x4x8 slice. The times are simulated.
256 devices in a mesh: dp: 32 (over z, y), expert: 8 (over x, core).
Axes of the slice: x: 4, y: 4, z: 8, core: 2. Of those that a mesh axis runs over, the one named last changes fastest.
Arguments:
- residual: bfloat16 [2048, 4096], P(('dp', 'expert')), may hold values from -8.2 to 8.2
- queries: bfloat16 [2048, 4096], P('dp', 'expert'), may hold values from -24 to 24
- new_keys: bfloat16 [2048, 1024], P('dp', 'expert'), may hold values from -6 to 6
- new_values: bfloat16 [2048, 1024], P('dp', 'expert'), may hold values from -6 to 6
- cache_keys: bfloat16 [64, 1024, 1024], P('dp', None, 'expert'), may hold values from -8 to 8
- cache_values: bfloat16 [64, 1024, 1024], P('dp', None, 'expert'), may hold values from -6 to 6
- out_weight: bfloat16 [4096, 4096], P('expert', 'dp'), may hold values from -1 to 1
- ffn_gain: float32 [4096], replicated, may hold values from 0.1 to 1.9
- router: bfloat16 [4096, 8], replicated, may hold values from -0.0234375 to 0.0234375
- routes: int32 [2048, 2], P(('dp', 'expert')), may hold values from 0 to 7, all different within a row; in each aligned block of 64 rows (0 to 63, 64 to 127, ...) at most 24 rows name the same one
- w_gate: bfloat16 [8, 4096, 14336], P('expert', None, 'dp'), may hold values from -0.09375 to 0.09375
- w_up: bfloat16 [8, 4096, 14336], P('expert', None, 'dp'), may hold values from -0.09375 to 0.09375
- w_down: bfloat16 [8, 14336, 4096], P('expert', 'dp'), may hold values from -0.046875 to 0.046875
- summary_gain: float32 [4096], P('expert'), may hold values from 0.1 to 1.9
- reduce_scale: float32 [32], P('expert'), may hold values from 0.1 to 30
- assign: int32 [64], replicated, may hold values from 0 to 3
Outputs:
- summary: bfloat16 [64, 4096], P('dp', 'expert')
- reduced: bfloat16 [64, 4096], P('dp', 'expert')
Inputs may be any that keep to these rules, and one draw needn't show every extreme that they name: `routes`: each token names 2 different experts and every expert is named by some token; among the tokens of one dp index (aligned blocks of 64 rows) no expert is named by more than 24 tokens, and that bound is reached in some block.
All inputs are finite; a program needn't handle non-finite values.
Results may differ from a plain program's by a relative error of at most 0.017.
Values may be sent and summed in bfloat16 or wider, within the bound.
No kernel may reach another device: no remote copies, remote signals or barrier semaphores. Data moves between devices by JAX's collectives and lax.ppermute only.
A program may use at most 128 MiB of HBM per device.

v0:
```python
import math
import jax
import jax.numpy as jnp
from jax import lax
from jax.sharding import PartitionSpec as P

HEADS = 32
KVH = 8
HD = 128
EXPERTS = 8
WIN = 32
GROUP_CAP = 24
EPSILON = 1e-05


def attend(queries, new_keys, new_values, cache_keys, cache_values):
    span_count, cache_len, kv_width = cache_keys.shape
    kv_local = kv_width // HD
    group = HEADS // KVH
    window = queries.shape[0] // span_count
    query_view = queries.reshape(span_count, window, kv_local, group, HD)
    fresh_keys = new_keys.reshape(span_count, window, kv_local, HD)
    fresh_values = new_values.reshape(span_count, window, kv_local, HD)
    stored_keys = cache_keys.reshape(span_count, cache_len, kv_local, HD)
    stored_values = cache_values.reshape(span_count, cache_len, kv_local, HD)
    factor = 1.0 / math.sqrt(HD)
    past_scores = (
        jnp.einsum("ctkgd,cpkd->ckgtp", query_view, stored_keys, preferred_element_type=jnp.float32)
        * factor
    )
    fresh_scores = (
        jnp.einsum("ctkgd,cskd->ckgts", query_view, fresh_keys, preferred_element_type=jnp.float32)
        * factor
    )
    causal = jnp.arange(window)[:, None] >= jnp.arange(window)[None, :]
    fresh_scores = jnp.where(causal, fresh_scores, -jnp.inf)
    highest = jnp.maximum(jnp.max(past_scores, axis=-1), jnp.max(fresh_scores, axis=-1))[..., None]
    past_exp = jnp.exp(past_scores - highest)
    fresh_exp = jnp.exp(fresh_scores - highest)
    totals = jnp.sum(past_exp, axis=-1, keepdims=True) + jnp.sum(fresh_exp, axis=-1, keepdims=True)
    past_weights = (past_exp / totals).astype(jnp.bfloat16)
    fresh_weights = (fresh_exp / totals).astype(jnp.bfloat16)
    context = jnp.einsum(
        "ckgtp,cpkd->ctkgd", past_weights, stored_values, preferred_element_type=jnp.float32
    )
    context = context + jnp.einsum(
        "ckgts,cskd->ctkgd", fresh_weights, fresh_values, preferred_element_type=jnp.float32
    )
    return context.astype(jnp.bfloat16).reshape(span_count * window, kv_local * group * HD)


def expert_rows(rows, w_gate, w_up, w_down):
    gate_proj = jnp.einsum("ned,edf->nef", rows, w_gate, preferred_element_type=jnp.float32)
    up_proj = jnp.einsum("ned,edf->nef", rows, w_up, preferred_element_type=jnp.float32)
    hidden = (jax.nn.silu(gate_proj) * up_proj).astype(jnp.bfloat16)
    return jnp.einsum("nef,efd->ned", hidden, w_down, preferred_element_type=jnp.float32)


def shards(
    residual,
    queries,
    new_keys,
    new_values,
    cache_keys,
    cache_values,
    out_weight,
    ffn_gain,
    router,
    routes,
    w_gate,
    w_up,
    w_down,
    summary_gain,
    reduce_scale,
    assign,
):
    expert_count = lax.axis_size("expert")
    dp_index = lax.axis_index("dp")
    column = lax.axis_index("expert")
    span_local = cache_keys.shape[0]
    tok_local = residual.shape[0]
    width = residual.shape[1]
    slice_width = width // expert_count
    highest_precision = lax.Precision.HIGHEST
    attended = attend(queries, new_keys, new_values, cache_keys, cache_values)
    head_terms = jnp.dot(
        attended,
        lax.all_gather(out_weight, "dp", axis=1, tiled=True),
        preferred_element_type=jnp.float32,
    )
    mixed = residual.astype(jnp.float32) + lax.psum_scatter(
        head_terms, "expert", scatter_dimension=0, tiled=True
    )
    normed = (
        mixed * lax.rsqrt(jnp.mean(mixed * mixed, axis=-1, keepdims=True) + EPSILON) * ffn_gain
    ).astype(jnp.bfloat16)
    logits = jnp.dot(normed, router, preferred_element_type=jnp.float32)
    expert_ids = jnp.arange(EXPERTS, dtype=jnp.int32)
    first = routes[:, 0:1] == expert_ids[None, :]
    second = routes[:, 1:2] == expert_ids[None, :]
    first_logit = jnp.sum(jnp.where(first, logits, 0.0), axis=-1)
    second_logit = jnp.sum(jnp.where(second, logits, 0.0), axis=-1)
    partner = jnp.where(first, routes[:, 1:2], jnp.where(second, routes[:, 0:1], -1))
    outgoing = jnp.where((partner >= 0).T[:, :, None], normed[None, :, :], 0)
    arrived_rows, arrived_partner = (
        lax.all_to_all(outgoing, "expert", split_axis=0, concat_axis=1, tiled=True),
        lax.all_to_all(partner.T, "expert", split_axis=0, concat_axis=1, tiled=True),
    )
    present = (arrived_partner >= 0).astype(jnp.int32)
    position = jnp.cumsum(present, axis=1) - 1
    picker = (present[:, None, :] > 0) & (
        position[:, None, :] == jnp.arange(GROUP_CAP)[None, :, None]
    )
    compact = jnp.einsum(
        "eks,esd->ked",
        picker.astype(jnp.bfloat16),
        arrived_rows,
        preferred_element_type=jnp.float32,
    ).astype(jnp.bfloat16)
    token_span = (column * tok_local + jnp.arange(tok_local)) // WIN
    pool_matrix = (token_span[None, :] == jnp.arange(span_local)[:, None]).astype(jnp.float32)
    gathered = lax.all_gather(compact, "dp", axis=0, tiled=True)
    returned = lax.psum_scatter(
        expert_rows(gathered, w_gate, w_up, w_down), "dp", scatter_dimension=0, tiled=True
    )
    spread = jnp.einsum(
        "eks,ked->esd", picker.astype(jnp.float32), returned, precision=highest_precision
    )
    back = lax.all_to_all(spread, "expert", split_axis=1, concat_axis=0, tiled=True)
    gate_table = jnp.where(first, jax.nn.sigmoid(first_logit - second_logit)[:, None], 0.0)
    gate_table = gate_table + jnp.where(
        second, jax.nn.sigmoid(second_logit - first_logit)[:, None], 0.0
    )
    token_out = mixed + jnp.einsum("te,etd->td", gate_table, back, precision=highest_precision)
    pooled_local = jnp.dot(pool_matrix, token_out, precision=highest_precision)
    pooled = lax.psum_scatter(pooled_local, "expert", scatter_dimension=1, tiled=True)
    squares = lax.psum(jnp.sum(pooled * pooled, axis=-1), "expert")
    summary = (pooled * lax.rsqrt(squares / width + EPSILON)[:, None] * summary_gain).astype(
        jnp.bfloat16
    )
    everyone = lax.all_gather(summary, "dp", axis=0, tiled=True)
    heads_local = slice_width // HD
    mine = summary.reshape(span_local, heads_local, HD)
    others = everyone.reshape(everyone.shape[0], heads_local, HD)
    factor = reduce_scale / math.sqrt(HD)
    scores = (
        jnp.einsum("chd,khd->hck", mine, others, preferred_element_type=jnp.float32)
        * factor[:, None, None]
    )
    own_assign = lax.dynamic_slice_in_dim(assign, dp_index * span_local, span_local)
    same = own_assign[:, None] == assign[None, :]
    scores = jnp.where(same[None], scores, -jnp.inf)
    highest = jnp.max(scores, axis=-1, keepdims=True)
    expo = jnp.exp(scores - highest)
    weights = (expo / jnp.sum(expo, axis=-1, keepdims=True)).astype(jnp.bfloat16)
    reduced = jnp.einsum("hck,khd->chd", weights, others, preferred_element_type=jnp.float32)
    reduced = reduced.reshape(span_local, slice_width).astype(jnp.bfloat16)
    return (summary, reduced)


def solution(mesh):
    return jax.shard_map(
        shards,
        mesh=mesh,
        in_specs=(
            P(("dp", "expert"), None),
            P("dp", "expert"),
            P("dp", "expert"),
            P("dp", "expert"),
            P("dp", None, "expert"),
            P("dp", None, "expert"),
            P("expert", "dp"),
            P(),
            P(),
            P(("dp", "expert"), None),
            P("expert", None, "dp"),
            P("expert", None, "dp"),
            P("expert", "dp", None),
            P("expert"),
            P("expert"),
            P(),
        ),
        out_specs=(P("dp", "expert"), P("dp", "expert")),
        check_vma=False,
    )
```

profile of v0, /device:TPU:8, one launch (start us, length us, event | category | flops | bytes accessed | tf_op | source)
XLA Modules:
  0.0 635.6 jit_solution(1223442760722272505)
XLA Ops:
  9.2 1.0 fusion.83
  10.6 0.9 fusion.61
  12.0 84.5 %all-gather.4.cloned.1.call-done = bf16[512,4096]{1,0:T(8,128)(2,1)} async-done(((bf16[512,128]{1,0:T(8,128)(2,1)}), bf16[512,4096]{1,0:T(8,128)(2,1)}) %all-gather.4.cloned.1.call-update) | async-done | bytes 4194320 | tf_op jit(solution)/shard_map/all_gather | solution.py:88
  96.5 4.0 fusion.58
  101.1 4.3 all-to-all-start
  105.4 30.2 %reduce-scatter.6.cloned.1.call-done = f32[8,4096]{1,0:T(8,128)} async-done(((f32[64,4096]{1,0:T(8,128)}), f32[8,4096]{1,0:T(8,128)}) %reduce-scatter.6.cloned.1.call-update) | async-done | bytes 131088 | tf_op jit(solution)/shard_map/reduce_scatter | solution.py:91
  135.5 1.1 multiply_reduce_fusion
  136.6 1.0 multiply_convert_fusion
  138.5 3.5 all-to-all-start.1
  142.5 9.8 %all-to-all-done.1 = bf16[8,8,4096]{2,1,0:T(8,128)(2,1)S(1)} async-done(((bf16[8,8,4096]{2,1,0:T(8,128)(2,1)}), bf16[8,8,4096]{2,1,0:T(8,128)(2,1)S(1)}, u32[]{:S(2)}, u32[]{:S(2)}) %all-to-all-start.1) | async-done | bytes 524320 | tf_op jit(solution)/shard_map/all_to_all | solution.py:106
  153.4 86.4 %all-gather.6.cloned.1.call-done = bf16[768,1,4096]{2,0,1:T(8,128)(2,1)} async-done(((bf16[24,1,4096]{2,0,1:T(8,128)(2,1)}), bf16[768,1,4096]{2,0,1:T(8,128)(2,1)}) %all-gather.6.cloned.1.call-update) | async-done | bytes 6291472 | tf_op jit(solution)/shard_map/all_gather | solution.py:122
  239.8 6.9 %fusion.9 = f32[768,1,448]{0,2,1:T(8,128)S(1)} fusion(bf16[1,4096,448]{1,2,0:T(8,128)(2,1)} %param.26, bf16[768,1,4096]{2,0,1:T(8,128)(2,1)} %all-gather.6.cloned.1.call-done), kind=kOutput, calls=%fused_computation.13 | convolution fusion | flops 2818572288 | bytes 11337728 | tf_op jit(solution)/shard_map/ned,edf->nef/dot_general | solution.py:53
  246.7 17.8 %convolution_bitcast_fusion = f32[768,1,4096]{2,0,1:T(8,128)} fusion(bf16[1,448,4096]{2,1,0:T(8,128)(2,1)} %param.28, bf16[1,4096,448]{1,2,0:T(8,128)(2,1)} %param.27, bf16[768,1,4096]{2,0,1:T(8,128)(2,1)} %all-gather.6.cloned.1.call-done, f32[768,1,448]{0,2,1:T(8,128)S(1)} %fusion.9), kind=kOutput, calls=%fused_computation.1 | convolution fusion | flops 5639208960 | bytes 27590656 | tf_op jit(solution)/shard_map/nef,efd->ned/dot_general | solution.py:56
  264.6 236.8 %reduce-scatter.8.cloned.1.call-done = f32[24,1,4096]{2,0,1:T(8,128)} async-done(((f32[768,1,4096]{2,0,1:T(8,128)}), f32[24,1,4096]{2,0,1:T(8,128)}) %reduce-scatter.8.cloned.1.call-update) | async-done | bytes 393232 | tf_op jit(solution)/shard_map/reduce_scatter | solution.py:123
  501.4 1.6 convolution_bitcast_fusion.2
  503.0 2.1 copy.45
  505.1 4.3 all-to-all-start.2
  510.0 15.3 %all-to-all-done.2 = f32[1,64,4096]{2,0,1:T(1,128)S(1)} async-done(((f32[1,64,4096]{2,0,1:T(1,128)}), f32[1,64,4096]{2,0,1:T(1,128)S(1)}, u32[]{:S(2)}, u32[]{:S(2)}) %all-to-all-start.2) | async-done | bytes 1048608 | tf_op jit(solution)/shard_map/all_to_all | solution.py:129
  525.9 1.5 fusion.47
  527.4 3.2 convolution_bitcast_fusion.1
  530.7 34.0 %reduce-scatter.10.cloned.1.call-done = f32[512,2]{1,0:T(8,128)} async-done(((f32[4096,2]{1,0:T(8,128)}), f32[512,2]{1,0:T(8,128)}) %reduce-scatter.10.cloned.1.call-update) | async-done | bytes 4112
  564.6 1.1 copy.58
  565.8 12.9 %psum.7 = f32[2]{0:T(128)S(1)} all-reduce(f32[2]{0:T(128)S(1)} %multiply_reduce_fusion.1), channel_id=1, replica_groups=mesh['dp'=32,'expert'=8] {'expert'}, use_global_device_ids=true, to_apply=%region_12.13 | all-reduce | flops 2 | bytes 16 | tf_op jit(solution)/shard_map/psum | solution.py:137
  578.9 49.0 %all-gather = bf16[32,2,512]{2,1,0:T(2,128)(2,1)S(1)} all-gather(bf16[1,2,512]{2,1,0:T(2,128)(2,1)S(1)} %fusion.95), channel_id=1, replica_groups=mesh['dp'=32,'expert'=8] {'dp'}, dimensions={0}, use_global_device_ids=true | all-gather | bytes 67584 | tf_op jit(solution)/shard_map/all_gather | solution.py:141
  (70 shorter events, 8.7 us)
Async XLA Ops:
  7.2 1.7 copy-start
  7.2 4.3 copy-start.8
  7.2 89.3 %all-gather.4.cloned.1.call-start = ((), (), s32[]{:S(2)}) async-start(), calls=%async_computation.6 | async-start | bytes 4325376 | tf_op jit(solution)/shard_map/all_gather | solution.py:88
  7.9 127.6 %reduce-scatter.6.cloned.1.call-start = ((), (), s32[]{:S(2)}) async-start(), calls=%async_computation.7 | async-start | bytes 1179648 | tf_op jit(solution)/shard_map/reduce_scatter | solution.py:91
  11.9 88.6 %copy-start.7 = (s32[8,2]{0,1:T(2,128)S(1)}, s32[8,2]{0,1:T(2,128)}, u32[]{:S(2)}) copy-start(s32[8,2]{0,1:T(2,128)} %param.25) | copy-start | bytes 196
  11.9 123.6 %copy-start.2 = (bf16[8,4096]{1,0:T(8,128)(2,1)S(1)}, bf16[8,4096]{1,0:T(8,128)(2,1)}, u32[]{:S(2)}) copy-start(bf16[8,4096]{1,0:T(8,128)(2,1)} %param.16) | copy-start | bytes 196612
  11.9 124.7 %copy-start.4 = (f32[4096]{0:T(1024)S(1)}, f32[4096]{0:T(1024)}, u32[]{:S(2)}) copy-start(f32[4096]{0:T(1024)} %param.23) | copy-start | bytes 49156
  101.1 37.4 %all-to-all-start = ((s32[8,1,8]{2,1,0:T(1,128)}), s32[8,1,8]{2,1,0:T(1,128)S(1)}, u32[]{:S(2)}, u32[]{:S(2)}) async-start(s32[8,1,8]{2,1,0:T(1,128)} %compare_select_fusion.1), calls=%async_computation.1 | async-start | bytes 8192 | tf_op jit(solution)/shard_map/all_to_all | solution.py:107
  138.5 13.7 %all-to-all-start.1 = ((bf16[8,8,4096]{2,1,0:T(8,128)(2,1)}), bf16[8,8,4096]{2,1,0:T(8,128)(2,1)S(1)}, u32[]{:S(2)}, u32[]{:S(2)}) async-start(bf16[8,8,4096]{2,1,0:T(8,128)(2,1)} %broadcast_select_fusion), calls=%async_computation.2 | async-start | bytes 1048576 | tf_op jit(solution)/shard_map/all_to_all | solution.py:106
  142.0 97.8 %all-gather.6.cloned.1.call-start = ((), (), s32[]{:S(2)}) async-start(), calls=%async_computation.8 | async-start | bytes 6488064 | tf_op jit(solution)/shard_map/all_gather | solution.py:122
  153.1 348.2 %reduce-scatter.8.cloned.1.call-start = ((), (), s32[]{:S(2)}) async-start(), calls=%async_computation.9 | async-start | bytes 12976128 | tf_op jit(solution)/shard_map/reduce_scatter | solution.py:123
  264.5 245.1 %copy-start.9 = (s32[64]{0:T(128)S(1)}, s32[64]{0:T(128)}, u32[]{:S(2)}) copy-start(s32[64]{0:T(128)} %param.31) | copy-start | bytes 772
  264.6 245.1 %copy-start.3 = (bf16[4096,8]{0,1:T(8,128)(2,1)S(1)}, bf16[4096,8]{0,1:T(8,128)(2,1)}, u32[]{:S(2)}) copy-start(bf16[4096,8]{0,1:T(8,128)(2,1)} %param.24) | copy-start | bytes 196612
  503.0 24.4 %copy-start.1 = (f32[8,4096]{1,0:T(8,128)S(1)}, f32[8,4096]{1,0:T(8,128)}, u32[]{:S(2)}) copy-start(f32[8,4096]{1,0:T(8,128)} %reduce-scatter.6.cloned.1.call-done) | copy-start | bytes 393220
  505.1 20.2 %all-to-all-start.2 = ((f32[1,64,4096]{2,0,1:T(1,128)}), f32[1,64,4096]{2,0,1:T(1,128)S(1)}, u32[]{:S(2)}, u32[]{:S(2)}) async-start(f32[1,64,4096]{2,0,1:T(1,128)} %copy.45), calls=%async_computation.4 | async-start | bytes 2097152 | tf_op jit(solution)/shard_map/all_to_all | solution.py:129
  509.3 55.3 %reduce-scatter.10.cloned.1.call-start = ((), (), s32[]{:S(2)}) async-start(), calls=%async_computation.10 | async-start | bytes 2359296
  510.0 55.9 %copy-start.10 = (f32[4]{0:T(128)S(1)}, f32[4]{0:T(128)}, u32[]{:S(2)}) copy-start(f32[4]{0:T(128)} %param.30) | copy-start | bytes 52
  510.0 68.8 %copy-start.5 = (f32[512]{0:T(512)S(1)}, f32[512]{0:T(512)}, u32[]{:S(2)}) copy-start(f32[512]{0:T(512)} %param.29) | copy-start | bytes 6148
  578.8 50.3 %copy-start.6 = (bf16[2,512]{1,0:T(2,128)(2,1)}, bf16[2,512]{1,0:T(2,128)(2,1)S(1)}, u32[]{:S(2)}) copy-start(bf16[2,512]{1,0:T(2,128)(2,1)S(1)} %multiply_convert_fusion.1) | copy-start | bytes 6148
Sparse Core Ops, SparseCore 0:
  10.5 85.9 all-gather.3
  100.6 34.8 reduce-scatter.5
  153.3 86.4 all-gather.5
  264.7 236.6 reduce-scatter.7
  530.7 33.8 reduce-scatter.9
where the time goes:
time: 636 us
  waiting for transfers between devices  498 us (78%)
  blocking collectives  61.9 us (10%)
  matrix products  39.8 us (6%)
  between operations  14.1 us (2%)
  starting transfers between devices  12.6 us (2%)
    reduce_scatter x1, waiting for transfers between devices, shards(): lax.psum_scatter(expert_rows(gathered, w_gate, w_up, w_down), 'dp', scatt...  237 us
    all_gather x1, waiting for transfers between devices, shards(): gathered = lax.all_gather(compact, 'dp', axis=0, tiled=True)  86.4 us
    all_gather x1, waiting for transfers between devices, shards(): lax.all_gather(out_weight, 'dp', axis=1, tiled=True)  84.5 us
    all_gather x1, blocking collectives, shards(): everyone = lax.all_gather(summary, 'dp', axis=0, tiled=True)  49 us
    unnamed x6, waiting for transfers between devices  34.7 us
    reduce_scatter x1, waiting for transfers between devices, shards(): lax.psum_scatter(head_terms, 'expert', scatter_dimension=0, tiled=True)  30.2 us
    dot_general x1, matrix products, expert_rows(): jnp.einsum('nef,efd->ned', hidden, w_down, preferred_element_type=jnp.flo...  17.8 us
    all_to_all x1, waiting for transfers between devices, shards(): lax.all_to_all(spread, 'expert', split_axis=1, concat_axis=0, tiled=True)  15.3 us
  transfers between devices with their start and end apart: 8, of which 7 were waited for; matrix products, arithmetic and copies ran while one was open for 1% of the time, Pallas kernels for 0%

commit v1 on v0

--- a/solution.py
+++ b/solution.py
@@ -119,7 +119,8 @@
     ).astype(jnp.bfloat16)
     token_span = (column * tok_local + jnp.arange(tok_local)) // WIN
     pool_matrix = (token_span[None, :] == jnp.arange(span_local)[:, None]).astype(jnp.float32)
-    gathered = lax.all_gather(compact, "dp", axis=0, tiled=True)
+    sent = jnp.stack([compact] * lax.axis_size("dp"))
+    gathered = jnp.concatenate(lax.all_to_all(sent, "dp", 0, 0), axis=0)
     returned = lax.psum_scatter(
         expert_rows(gathered, w_gate, w_up, w_down), "dp", scatter_dimension=0, tiled=True
     )

time: 636 us -> 695 us (1.093)
  blocking collectives: 61.9 us -> 212 us
  waiting for transfers between devices: 498 us -> 408 us
    all_to_all x0 -> x1, blocking collectives: none -> 150 us  [shards(): gathered = jnp.concatenate(lax.all_to_all(sent, 'dp', 0, 0), axis=0)]
    all_gather x1 -> x0, waiting for transfers between devices: 86.4 us -> none  [shards(): gathered = lax.all_gather(compact, 'dp', axis=0, tiled=True)]
    unnamed x6 -> x5, waiting for transfers between devices: 34.7 us -> 34.7 us
  transfers between devices with their start and end apart: 8 -> 7, of which waited for: 7 -> 6; matrix products, arithmetic and copies ran while one was open for 1% -> 1% of each run, Pallas kernels for 0% -> 0%
where the time goes in v1:
time: 695 us
  waiting for transfers between devices  408 us (59%)
  blocking collectives  212 us (31%)
  matrix products  35.3 us (5%)
  between operations  14.1 us (2%)
  starting transfers between devices  12.4 us (2%)
  local copies, waits for them, and re-layouts  8.43 us (1%)
    reduce_scatter x1, waiting for transfers between devices, shards(): lax.psum_scatter(expert_rows(gathered, w_gate, w_up, w_down), 'dp', scatt...  233 us
    all_to_all x1, blocking collectives, shards(): gathered = jnp.concatenate(lax.all_to_all(sent, 'dp', 0, 0), axis=0)  150 us
    all_gather x1, waiting for transfers between devices, shards(): lax.all_gather(out_weight, 'dp', axis=1, tiled=True)  84.5 us
    all_gather x1, blocking collectives, shards(): everyone = lax.all_gather(summary, 'dp', axis=0, tiled=True)  49 us
    unnamed x5, waiting for transfers between devices  34.7 us
    reduce_scatter x1, waiting for transfers between devices, shards(): lax.psum_scatter(head_terms, 'expert', scatter_dimension=0, tiled=True)  30.2 us
    dot_general x1, matrix products, expert_rows(): jnp.einsum('nef,efd->ned', hidden, w_down, preferred_element_type=jnp.flo...  17.9 us
    all_to_all x1, waiting for transfers between devices, shards(): lax.all_to_all(spread, 'expert', split_axis=1, concat_axis=0, tiled=True)  15.3 us
  transfers between devices with their start and end apart: 7, of which 6 were waited for; matrix products, arithmetic and copies ran while one was open for 1% of the time, Pallas kernels for 0%

profile of v1, /device:TPU:8, one launch (start us, length us, event | category | flops | bytes accessed | tf_op | source)
XLA Modules:
  0.0 694.8 jit_solution(9949856112654765376)
XLA Ops:
  9.2 1.0 fusion.69
  12.0 84.5 %all-gather.3.cloned.1.call-done = bf16[512,4096]{1,0:T(8,128)(2,1)} async-done(((bf16[512,128]{1,0:T(8,128)(2,1)}), bf16[512,4096]{1,0:T(8,128)(2,1)}) %all-gather.3.cloned.1.call-update) | async-done | bytes 4194320 | tf_op jit(solution)/shard_map/all_gather | solution.py:88
  96.5 4.0 fusion.44
  101.1 4.3 all-to-all-start
  105.4 30.2 %reduce-scatter.6.cloned.1.call-done = f32[8,4096]{1,0:T(8,128)} async-done(((f32[64,4096]{1,0:T(8,128)}), f32[8,4096]{1,0:T(8,128)}) %reduce-scatter.6.cloned.1.call-update) | async-done | bytes 131088 | tf_op jit(solution)/shard_map/reduce_scatter | solution.py:91
  135.5 1.1 multiply_reduce_fusion
  136.6 1.0 multiply_convert_fusion
  138.5 3.5 all-to-all-start.1
  142.5 9.8 %all-to-all-done.1 = bf16[8,8,4096]{2,1,0:T(8,128)(2,1)S(1)} async-done(((bf16[8,8,4096]{2,1,0:T(8,128)(2,1)}), bf16[8,8,4096]{2,1,0:T(8,128)(2,1)S(1)}, u32[]{:S(2)}, u32[]{:S(2)}) %all-to-all-start.1) | async-done | bytes 524320 | tf_op jit(solution)/shard_map/all_to_all | solution.py:106
  153.2 150.4 %all_to_all.36 = bf16[32,24,1,4096]{3,1,2,0:T(8,128)(2,1)S(1)} all-to-all(bf16[32,24,1,4096]{3,1,2,0:T(8,128)(2,1)S(1)} %stack.2), channel_id=1, replica_groups=mesh['dp'=32,'expert'=8] {'dp'}, dimensions={0} | all-to-all | bytes 12582912 | tf_op jit(solution)/shard_map/all_to_all | solution.py:123
  303.7 2.6 copy-done.1
  306.3 3.1 fusion.7
  309.3 17.9 %convolution_bitcast_fusion = f32[768,1,4096]{2,0,1:T(8,128)} fusion(bf16[1,448,4096]{2,1,0:T(8,128)(2,1)} %param.28, bf16[768,4096]{1,0:T(8,128)(2,1)} %bitcast.151, bf16[1,4096,448]{1,2,0:T(8,128)(2,1)} %param.27, f32[768,1,448]{0,2,1:T(8,128)S(1)} %fusion.7), kind=kOutput, calls=%fused_computation.1 | convolution fusion | flops 5639208960 | bytes 27590656 | tf_op jit(solution)/shard_map/nef,efd->ned/dot_general | solution.py:56
  327.2 233.3 %reduce-scatter.8.cloned.1.call-done = f32[24,1,4096]{2,0,1:T(8,128)} async-done(((f32[768,1,4096]{2,0,1:T(8,128)}), f32[24,1,4096]{2,0,1:T(8,128)}) %reduce-scatter.8.cloned.1.call-update) | async-done | bytes 393232 | tf_op jit(solution)/shard_map/reduce_scatter | solution.py:124
  560.5 1.6 convolution_bitcast_fusion.2
  562.1 2.1 copy.45
  564.2 4.3 all-to-all-start.3
  569.1 15.3 %all-to-all-done.3 = f32[1,64,4096]{2,0,1:T(1,128)S(1)} async-done(((f32[1,64,4096]{2,0,1:T(1,128)}), f32[1,64,4096]{2,0,1:T(1,128)S(1)}, u32[]{:S(2)}, u32[]{:S(2)}) %all-to-all-start.3) | async-done | bytes 1048608 | tf_op jit(solution)/shard_map/all_to_all | solution.py:130
  585.0 1.5 fusion.33
  586.5 3.2 convolution_bitcast_fusion.1
  589.8 34.0 %reduce-scatter.10.cloned.1.call-done = f32[512,2]{1,0:T(8,128)} async-done(((f32[4096,2]{1,0:T(8,128)}), f32[512,2]{1,0:T(8,128)}) %reduce-scatter.10.cloned.1.call-update) | async-done | bytes 4112
  623.8 1.1 copy.58
  625.0 12.9 %psum.7 = f32[2]{0:T(128)S(1)} all-reduce(f32[2]{0:T(128)S(1)} %multiply_reduce_fusion.1), channel_id=1, replica_groups=mesh['dp'=32,'expert'=8] {'expert'}, use_global_device_ids=true, to_apply=%region_12.13 | all-reduce | flops 2 | bytes 16 | tf_op jit(solution)/shard_map/psum | solution.py:138
  638.1 49.0 %all-gather = bf16[32,2,512]{2,1,0:T(2,128)(2,1)S(1)} all-gather(bf16[1,2,512]{2,1,0:T(2,128)(2,1)S(1)} %fusion.83), channel_id=1, replica_groups=mesh['dp'=32,'expert'=8] {'dp'}, dimensions={0}, use_global_device_ids=true | all-gather | bytes 67584 | tf_op jit(solution)/shard_map/all_gather | solution.py:142
  (73 shorter events, 9.5 us)
Async XLA Ops:
  7.2 1.7 copy-start
  7.2 4.3 copy-start.10
  7.2 89.3 %all-gather.3.cloned.1.call-start = ((), (), s32[]{:S(2)}) async-start(), calls=%async_computation.7 | async-start | bytes 4325376 | tf_op jit(solution)/shard_map/all_gather | solution.py:88
  7.9 127.6 %reduce-scatter.6.cloned.1.call-start = ((), (), s32[]{:S(2)}) async-start(), calls=%async_computation.8 | async-start | bytes 1179648 | tf_op jit(solution)/shard_map/reduce_scatter | solution.py:91
  11.9 88.6 %copy-start.8 = (s32[8,2]{0,1:T(2,128)S(1)}, s32[8,2]{0,1:T(2,128)}, u32[]{:S(2)}) copy-start(s32[8,2]{0,1:T(2,128)} %param.25) | copy-start | bytes 196
  11.9 123.6 %copy-start.3 = (bf16[8,4096]{1,0:T(8,128)(2,1)S(1)}, bf16[8,4096]{1,0:T(8,128)(2,1)}, u32[]{:S(2)}) copy-start(bf16[8,4096]{1,0:T(8,128)(2,1)} %param.16) | copy-start | bytes 196612
  11.9 124.7 %copy-start.5 = (f32[4096]{0:T(1024)S(1)}, f32[4096]{0:T(1024)}, u32[]{:S(2)}) copy-start(f32[4096]{0:T(1024)} %param.23) | copy-start | bytes 49156
  101.1 37.4 %all-to-all-start = ((s32[8,1,8]{2,1,0:T(1,128)}), s32[8,1,8]{2,1,0:T(1,128)S(1)}, u32[]{:S(2)}, u32[]{:S(2)}) async-start(s32[8,1,8]{2,1,0:T(1,128)} %compare_select_fusion.1), calls=%async_computation.1 | async-start | bytes 8192 | tf_op jit(solution)/shard_map/all_to_all | solution.py:107
  138.5 13.7 %all-to-all-start.1 = ((bf16[8,8,4096]{2,1,0:T(8,128)(2,1)}), bf16[8,8,4096]{2,1,0:T(8,128)(2,1)S(1)}, u32[]{:S(2)}, u32[]{:S(2)}) async-start(bf16[8,8,4096]{2,1,0:T(8,128)(2,1)} %broadcast_select_fusion), calls=%async_computation.2 | async-start | bytes 1048576 | tf_op jit(solution)/shard_map/all_to_all | solution.py:106
  142.0 418.5 %reduce-scatter.8.cloned.1.call-start = ((), (), s32[]{:S(2)}) async-start(), calls=%async_computation.9 | async-start | bytes 12976128 | tf_op jit(solution)/shard_map/reduce_scatter | solution.py:124
  153.2 153.0 %copy-start.9 = (bf16[1,4096,448]{1,2,0:T(8,128)(2,1)S(1)}, bf16[1,4096,448]{1,2,0:T(8,128)(2,1)}, u32[]{:S(2)}) copy-start(bf16[1,4096,448]{1,2,0:T(8,128)(2,1)} %param.26) | copy-start | bytes 11010052
  303.7 2.6 copy-start.1
  327.2 241.5 %copy-start.11 = (s32[64]{0:T(128)S(1)}, s32[64]{0:T(128)}, u32[]{:S(2)}) copy-start(s32[64]{0:T(128)} %param.31) | copy-start | bytes 772
  327.2 241.6 %copy-start.4 = (bf16[4096,8]{0,1:T(8,128)(2,1)S(1)}, bf16[4096,8]{0,1:T(8,128)(2,1)}, u32[]{:S(2)}) copy-start(bf16[4096,8]{0,1:T(8,128)(2,1)} %param.24) | copy-start | bytes 196612
  562.1 24.4 %copy-start.2 = (f32[8,4096]{1,0:T(8,128)S(1)}, f32[8,4096]{1,0:T(8,128)}, u32[]{:S(2)}) copy-start(f32[8,4096]{1,0:T(8,128)} %reduce-scatter.6.cloned.1.call-done) | copy-start | bytes 393220
  564.2 20.2 %all-to-all-start.3 = ((f32[1,64,4096]{2,0,1:T(1,128)}), f32[1,64,4096]{2,0,1:T(1,128)S(1)}, u32[]{:S(2)}, u32[]{:S(2)}) async-start(f32[1,64,4096]{2,0,1:T(1,128)} %copy.45), calls=%async_computation.5 | async-start | bytes 2097152 | tf_op jit(solution)/shard_map/all_to_all | solution.py:130
  568.5 55.3 %reduce-scatter.10.cloned.1.call-start = ((), (), s32[]{:S(2)}) async-start(), calls=%async_computation.10 | async-start | bytes 2359296
  569.1 55.9 %copy-start.12 = (f32[4]{0:T(128)S(1)}, f32[4]{0:T(128)}, u32[]{:S(2)}) copy-start(f32[4]{0:T(128)} %param.30) | copy-start | bytes 52
  569.1 68.8 %copy-start.6 = (f32[512]{0:T(512)S(1)}, f32[512]{0:T(512)}, u32[]{:S(2)}) copy-start(f32[512]{0:T(512)} %param.29) | copy-start | bytes 6148
  638.0 50.3 %copy-start.7 = (bf16[2,512]{1,0:T(2,128)(2,1)}, bf16[2,512]{1,0:T(2,128)(2,1)S(1)}, u32[]{:S(2)}) copy-start(bf16[2,512]{1,0:T(2,128)(2,1)S(1)} %multiply_convert_fusion.1) | copy-start | bytes 6148
Sparse Core Ops, SparseCore 0:
  10.5 85.9 all-gather.2
  100.6 34.8 reduce-scatter.5
  327.3 233.1 reduce-scatter.7
  589.9 33.9 reduce-scatter.9
